TPU v7x, 32 devices: a whole 2x2x4 slice. The times are simulated.
32 devices in a mesh: tm: 8 (over z, x), state: 4 (over y, core).
Axes of the slice: x: 2, y: 2, z: 4, core: 2. Of those that a mesh axis runs over, the one named last changes fastest.
Arguments:
- obs: bfloat16 [2048, 16, 256], P(('state', 'tm')), may hold values from -6 to 6
- mask: int32 [2048, 16], P(('state', 'tm')), may hold values 0 or 1
- loadings: bfloat16 [2048, 2048], P('state'), may hold values from -0.125 to 0.125
- decay: float32 [16, 2048], P('tm', 'state'), may hold values from 0 to 1, as said below
Outputs:
- smoothed: float32 [2048, 16, 256], P('state', 'tm')
- residual: float32 [2048, 16, 256], P('state', 'tm')
Inputs may be any that keep to these rules, and one draw needn't show every extreme that they name: Every decay lies strictly between 0 and 1.
All inputs are finite; a program needn't handle non-finite values. No bound on the sum of `mask` on one device may be relied on, other than what follows from the above.
Results may differ from a plain program's by a relative error of at most 0.0021.
Values may be sent and summed in bfloat16 or wider, within the bound.
No kernel may reach another device: no remote copies, remote signals or barrier semaphores. Data moves between devices by JAX's collectives and lax.ppermute only.
A program may use at most 64 MiB of HBM per device.

v0:
```python
import jax
import jax.numpy as jnp
from jax import lax
from jax.sharding import PartitionSpec as P

CHUNKS = 2


def smooth_chunk(information, decay_all):
    comps, hours, width = information.shape
    state = jnp.zeros((comps, width), jnp.float32)
    filtered = []
    for hour in range(hours):
        state = decay_all[hour][:, None] * state + information[:, hour, :]
        filtered.append(state)
    state = jnp.zeros((comps, width), jnp.float32)
    rows = [None] * hours
    for hour in reversed(range(hours)):
        rate = decay_all[hour]
        state = rate[:, None] * state + (1.0 - rate * rate)[:, None] * filtered[hour]
        rows[hour] = state
    return jnp.stack(rows, axis=1)


def local(obs, mask, loadings, decay):
    tm_count = lax.axis_size("tm")
    tm_index = lax.axis_index("tm")
    _, hours, members = obs.shape
    chunk_members = members // CHUNKS
    masked = obs * mask[:, :, None].astype(obs.dtype)
    by_hour = lax.all_to_all(masked, "tm", split_axis=1, concat_axis=0, tiled=True)
    slab_hours, comps = decay.shape
    padded = jnp.zeros((tm_count, slab_hours, comps), jnp.float32)
    padded = lax.dynamic_update_slice(padded, decay[None], (tm_index, 0, 0))
    decay_all = lax.psum(padded, "tm").reshape(tm_count * slab_hours, comps)
    smoothed_parts = []
    residual_parts = []
    for chunk in range(CHUNKS):
        low = chunk * chunk_members
        piece = masked[:, :, low : low + chunk_members]
        by_member = lax.all_to_all(piece, "tm", split_axis=2, concat_axis=0, tiled=True)
        stations_here, _, width = by_member.shape
        partial = jnp.dot(
            loadings.T,
            by_member.reshape(stations_here, hours * width),
            preferred_element_type=jnp.float32,
        )
        information = lax.psum_scatter(partial, "state", scatter_dimension=0, tiled=True)
        information = information.reshape(information.shape[0], hours, width)
        smoothed_here = smooth_chunk(information, decay_all)
        smoothed = lax.all_to_all(smoothed_here, "tm", split_axis=1, concat_axis=2, tiled=True)
        rounded = smoothed.astype(jnp.bfloat16)
        fitted = jnp.einsum(
            "so,ogy->sgy",
            loadings,
            lax.all_gather(rounded, "state", axis=0, tiled=True),
            preferred_element_type=jnp.float32,
        )
        residual = by_hour[:, :, low : low + chunk_members].astype(jnp.float32) - fitted
        smoothed_parts.append(smoothed)
        residual_parts.append(residual)
    return (jnp.concatenate(smoothed_parts, axis=2), jnp.concatenate(residual_parts, axis=2))


def solution(mesh):
    return jax.shard_map(
        local,
        mesh=mesh,
        in_specs=(
            P(("state", "tm"), None, None),
            P(("state", "tm"), None),
            P("state", None),
            P("tm", "state"),
        ),
        out_specs=(P("state", "tm", None), P("state", "tm", None)),
        check_vma=False,
    )
```

profile of v0, /device:TPU:0, one launch (start us, length us, event | category | flops | bytes accessed | tf_op | source)
XLA Modules:
  0.0 196.1 jit_solution(5214605081453235125)
XLA Ops:
  8.1 3.5 %copy.34 = bf16[64,16,256]{0,1,2:T(8,128)(2,1)} copy(bf16[64,16,256]{2,1,0:T(8,128)(2,1)} %param.4) | data formatting | bytes 1048576 | tf_op args[0]
  14.0 1.4 reshape.7069
  15.5 16.1 %all_to_all.84 = bf16[8,2,8192]{2,1,0:T(2,128)(2,1)} all-to-all(bf16[8,2,8192]{2,1,0:T(2,128)(2,1)S(1)} %reshape.7069), channel_id=1, replica_groups=mesh['tm'=8,'state'=4] {'tm'}, dimensions={0} | all-to-all | bytes 524288 | tf_op jit(solution)/shard_map/all_to_all | solution.py:41
  31.6 2.1 %reshape.7070 = bf16[128,16,64]{2,1,0:T(8,128)(2,1)} reshape(bf16[8,2,8192]{2,1,0:T(2,128)(2,1)} %all_to_all.84) | data formatting | bytes 524288
  33.7 2.2 %copy.39 = bf16[8,64,16,16]{1,0,3,2:T(8,128)(2,1)} copy(bf16[8,64,16,16]{1,2,3,0:T(8,128)(2,1)} %bitcast.86) | data formatting | bytes 524288 | tf_op jit(solution)/shard_map/all_to_all | solution.py:41
  37.2 2.0 %convolution_bitcast_fusion = f32[2048,256]{0,1:T(8,128)} fusion(bf16[512,256]{0,1:T(8,128)(2,1)S(1)} %reshape.7066, bf16[512,2048]{1,0:T(8,128)(2,1)S(1)} %copy-done), kind=kOutput, calls=%fused_computation | convolution fusion | flops 536870912 | bytes 4456448 | tf_op jit(solution)/shard_map/dot_general | solution.py:43
  39.4 1.4 reshape.7071
  40.8 12.1 %all_to_all.85 = bf16[8,2,8192]{2,1,0:T(2,128)(2,1)} all-to-all(bf16[8,2,8192]{2,1,0:T(2,128)(2,1)S(1)} %reshape.7071), channel_id=1, replica_groups=mesh['tm'=8,'state'=4] {'tm'}, dimensions={0} | all-to-all | bytes 524288 | tf_op jit(solution)/shard_map/all_to_all | solution.py:41
  52.8 2.1 %reshape.7072 = bf16[128,16,64]{2,1,0:T(8,128)(2,1)} reshape(bf16[8,2,8192]{2,1,0:T(2,128)(2,1)} %all_to_all.85) | data formatting | bytes 524288
  55.0 2.3 %copy.36 = bf16[8,64,16,16]{1,0,3,2:T(8,128)(2,1)} copy(bf16[8,64,16,16]{1,2,3,0:T(8,128)(2,1)} %bitcast.87) | data formatting | bytes 524288 | tf_op jit(solution)/shard_map/all_to_all | solution.py:41
  58.6 2.1 %convolution_bitcast_fusion.1 = f32[2048,256]{0,1:T(8,128)} fusion(bf16[512,256]{0,1:T(8,128)(2,1)S(1)} %reshape.7064, bf16[512,2048]{1,0:T(8,128)(2,1)S(1)} %copy-done), kind=kOutput, calls=%fused_computation.1 | convolution fusion | flops 536870912 | bytes 4456448 | tf_op jit(solution)/shard_map/dot_general | solution.py:43
  61.4 35.2 %psum.7 = f32[16,512]{1,0:T(8,128)S(1)} all-reduce(f32[16,512]{1,0:T(8,128)S(1)} %reshape.7063), channel_id=1, replica_groups=mesh['tm'=8,'state'=4] {'tm'}, use_global_device_ids=true, to_apply=%region_0.0 | all-reduce | flops 8192 | bytes 65536 | tf_op jit(solution)/shard_map/psum | solution.py:35
  101.6 1.9 constant_dynamic-update-slice_fusion.31
  117.0 1.5 constant_dynamic-update-slice_fusion
  118.5 20.1 %all_to_all.86 = f32[512,16,16]{0,2,1:T(8,128)S(1)} all-to-all(f32[512,16,16]{0,2,1:T(8,128)} %get-tuple-element.61), channel_id=1, replica_groups=mesh['tm'=8,'state'=4] {'tm'}, dimensions={1} | all-to-all | bytes 1048576 | tf_op jit(solution)/shard_map/all_to_all | solution.py:51
  140.2 4.2 %all-to-all-start.1 = ((f32[512,16,16]{0,2,1:T(8,128)}), f32[512,16,16]{0,2,1:T(8,128)}, u32[]{:S(2)}, u32[]{:S(2)}) async-start(f32[512,16,16]{0,2,1:T(8,128)} %copy-done.3), calls=%async_computation.2 | async-start | bytes 1048576 | tf_op jit(solution)/shard_map/all_to_all | solution.py:51
  144.3 1.6 copy.41
  146.0 12.1 %all-to-all-done.1 = f32[512,16,16]{0,2,1:T(8,128)} async-done(((f32[512,16,16]{0,2,1:T(8,128)}), f32[512,16,16]{0,2,1:T(8,128)}, u32[]{:S(2)}, u32[]{:S(2)}) %all-to-all-start.1) | async-done | bytes 524320 | tf_op jit(solution)/shard_map/all_to_all | solution.py:51
  158.0 4.1 %all-to-all-start.4 = ((bf16[64,16,256]{2,0,1:T(8,128)(2,1)}), bf16[64,16,256]{2,0,1:T(8,128)(2,1)}, u32[]{:S(2)}, u32[]{:S(2)}) async-start(bf16[64,16,256]{2,0,1:T(8,128)(2,1)} %copy.41), calls=%async_computation.6 | async-start | bytes 1048576 | tf_op jit(solution)/shard_map/all_to_all | solution.py:31
  164.1 11.4 %all-to-all-done.4 = bf16[64,16,256]{2,0,1:T(8,128)(2,1)} async-done(((bf16[64,16,256]{2,0,1:T(8,128)(2,1)}), bf16[64,16,256]{2,0,1:T(8,128)(2,1)}, u32[]{:S(2)}, u32[]{:S(2)}) %all-to-all-start.4) | async-done | bytes 524320 | tf_op jit(solution)/shard_map/all_to_all | solution.py:31
  177.4 1.8 copy.49
  181.1 2.2 %copy.45 = f32[512,2,256]{2,1,0:T(2,128)} copy(f32[512,2,256]{0,2,1:T(8,128)} %pad_maximum_fusion) | data formatting | bytes 2097152
  183.4 2.8 %fusion.13 = f32[512,2,128]{0,2,1:T(8,128)} fusion(bf16[2048,2,128]{0,2,1:T(8,128)(2,1)} %all-gather.5.cloned.1.call-done, bf16[512,2048]{1,0:T(8,128)(2,1)S(1)} %copy-done, bf16[512,2,128]{0,2,1:T(8,128)(2,1)S(1)} %copy-done.6), kind=kOutput, calls=%fused_computation.9 | convolution fusion | flops 537133056 | bytes 3932160 | tf_op jit(solution)/shard_map/so,ogy->sgy/dot_general | solution.py:53
  186.2 2.0 %fusion.7 = f32[512,2,128]{0,2,1:T(8,128)S(1)} fusion(bf16[2048,2,128]{0,2,1:T(8,128)(2,1)} %all-gather.3.cloned.1.call-done, bf16[512,2048]{1,0:T(8,128)(2,1)S(1)} %copy-done, bf16[512,2,128]{0,2,1:T(8,128)(2,1)S(1)} %copy-done.5), kind=kOutput, calls=%fused_computation.7 | convolution fusion | flops 537133056 | bytes 3932160 | tf_op jit(solution)/shard_map/so,ogy->sgy/dot_general | solution.py:53
  (111 shorter events, 33.7 us)
Async XLA Ops:
  7.2 30.1 %copy-start = (bf16[512,2048]{1,0:T(8,128)(2,1)S(1)}, bf16[512,2048]{1,0:T(8,128)(2,1)}, u32[]{:S(2)}) copy-start(bf16[512,2048]{1,0:T(8,128)(2,1)} %param.6) | copy-start | bytes 6291460
  7.2 94.3 %reduce-scatter.5.cloned.1.call-start = ((), (), s32[]{:S(2)}) async-start(), calls=%async_computation.8 | async-start | bytes 2621440 | tf_op jit(solution)/shard_map/reduce_scatter | solution.py:48
  39.3 64.7 %reduce-scatter.3.cloned.1.call-start = ((), (), s32[]{:S(2)}) async-start(), calls=%async_computation.7 | async-start | bytes 2621440 | tf_op jit(solution)/shard_map/reduce_scatter | solution.py:48
  60.7 122.6 %all-gather.5.cloned.1.call-start = ((), (), s32[]{:S(2)}) async-start(), calls=%async_computation.10 | async-start | bytes 1310720 | tf_op jit(solution)/shard_map/all_gather | solution.py:56
  96.6 4.9 %copy-start.7 = (f32[1,512]{1,0:T(1,128)}, f32[1,512]{1,0:T(1,128)S(1)}, u32[]{:S(2)}) copy-start(f32[1,512]{1,0:T(1,128)S(1)} %get-tuple-element.50) | copy-start | bytes 6148
  96.6 4.9 %copy-start.9 = (f32[1,512]{1,0:T(1,128)}, f32[1,512]{1,0:T(1,128)S(1)}, u32[]{:S(2)}) copy-start(f32[1,512]{1,0:T(1,128)S(1)} %get-tuple-element.52) | copy-start | bytes 6148
  96.6 4.9 %copy-start.11 = (f32[1,512]{1,0:T(1,128)}, f32[1,512]{1,0:T(1,128)S(1)}, u32[]{:S(2)}) copy-start(f32[1,512]{1,0:T(1,128)S(1)} %get-tuple-element.54) | copy-start | bytes 6148
  96.7 4.9 %copy-start.12 = (f32[1,512]{1,0:T(1,128)}, f32[1,512]{1,0:T(1,128)S(1)}, u32[]{:S(2)}) copy-start(f32[1,512]{1,0:T(1,128)S(1)} %get-tuple-element.56) | copy-start | bytes 6148
  96.7 4.9 %copy-start.13 = (f32[1,512]{1,0:T(1,128)}, f32[1,512]{1,0:T(1,128)S(1)}, u32[]{:S(2)}) copy-start(f32[1,512]{1,0:T(1,128)S(1)} %get-tuple-element.58) | copy-start | bytes 6148
  96.7 4.9 %copy-start.17 = (f32[1,512]{1,0:T(1,128)}, f32[1,512]{1,0:T(1,128)S(1)}, u32[]{:S(2)}) copy-start(f32[1,512]{1,0:T(1,128)S(1)} %get-tuple-element.47) | copy-start | bytes 6148
  96.7 4.9 %copy-start.18 = (f32[1,512]{1,0:T(1,128)}, f32[1,512]{1,0:T(1,128)S(1)}, u32[]{:S(2)}) copy-start(f32[1,512]{1,0:T(1,128)S(1)} %get-tuple-element.49) | copy-start | bytes 6148
  96.7 4.9 %copy-start.19 = (f32[1,512]{1,0:T(1,128)}, f32[1,512]{1,0:T(1,128)S(1)}, u32[]{:S(2)}) copy-start(f32[1,512]{1,0:T(1,128)S(1)} %get-tuple-element.51) | copy-start | bytes 6148
  96.7 4.9 %copy-start.20 = (f32[1,512]{1,0:T(1,128)}, f32[1,512]{1,0:T(1,128)S(1)}, u32[]{:S(2)}) copy-start(f32[1,512]{1,0:T(1,128)S(1)} %get-tuple-element.53) | copy-start | bytes 6148
  96.7 4.9 %copy-start.21 = (f32[1,512]{1,0:T(1,128)}, f32[1,512]{1,0:T(1,128)S(1)}, u32[]{:S(2)}) copy-start(f32[1,512]{1,0:T(1,128)S(1)} %get-tuple-element.55) | copy-start | bytes 6148
  104.0 7.3 %copy-start.10 = (f32[1,512]{1,0:T(1,128)S(1)}, f32[1,512]{1,0:T(1,128)}, u32[]{:S(2)}) copy-start(f32[1,512]{1,0:T(1,128)} %copy-done.9) | copy-start | bytes 6148
  104.0 7.3 %copy-start.16 = (f32[512]{0:T(512)S(1)}, f32[512]{0:T(512)}, u32[]{:S(2)}) copy-start(f32[512]{0:T(512)} %get-tuple-element.86) | copy-start | bytes 6148
  104.0 8.6 %copy-start.8 = (f32[1,512]{1,0:T(1,128)S(1)}, f32[1,512]{1,0:T(1,128)}, u32[]{:S(2)}) copy-start(f32[1,512]{1,0:T(1,128)} %copy-done.7) | copy-start | bytes 6148
  104.0 8.6 %copy-start.15 = (f32[512]{0:T(512)S(1)}, f32[512]{0:T(512)}, u32[]{:S(2)}) copy-start(f32[512]{0:T(512)} %get-tuple-element.88) | copy-start | bytes 6148
  104.0 9.8 %copy-start.14 = (f32[512]{0:T(512)S(1)}, f32[512]{0:T(512)}, u32[]{:S(2)}) copy-start(f32[512]{0:T(512)} %get-tuple-element.90) | copy-start | bytes 6148
  118.5 20.1 %copy-start.3 = (f32[512,16,16]{0,2,1:T(8,128)}, f32[512,16,16]{0,2,1:T(8,128)S(1)}, u32[]{:S(2)}) copy-start(f32[512,16,16]{0,2,1:T(8,128)S(1)} %get-tuple-element.60) | copy-start | bytes 1572868
  140.2 17.9 %all-to-all-start.1 = ((f32[512,16,16]{0,2,1:T(8,128)}), f32[512,16,16]{0,2,1:T(8,128)}, u32[]{:S(2)}, u32[]{:S(2)}) async-start(f32[512,16,16]{0,2,1:T(8,128)} %copy-done.3), calls=%async_computation.2 | async-start | bytes 1048576 | tf_op jit(solution)/shard_map/all_to_all | solution.py:51
  158.0 17.5 %all-to-all-start.4 = ((bf16[64,16,256]{2,0,1:T(8,128)(2,1)}), bf16[64,16,256]{2,0,1:T(8,128)(2,1)}, u32[]{:S(2)}, u32[]{:S(2)}) async-start(bf16[64,16,256]{2,0,1:T(8,128)(2,1)} %copy.41), calls=%async_computation.6 | async-start | bytes 1048576 | tf_op jit(solution)/shard_map/all_to_all | solution.py:31
  162.2 24.0 %all-gather.3.cloned.1.call-start = ((), (), s32[]{:S(2)}) async-start(), calls=%async_computation.9 | async-start | bytes 1310720 | tf_op jit(solution)/shard_map/all_gather | solution.py:56
  163.3 16.7 %copy-start.2 = (f32[512,8,2,16]{0,3,1,2:T(8,128)S(1)}, f32[512,8,2,16]{0,3,1,2:T(8,128)}, u32[]{:S(2)}) copy-start(f32[512,8,2,16]{0,3,1,2:T(8,128)} %copy-done.1) | copy-start | bytes 1572868
  (7 other events, 19.4 us)
Sparse Core Ops, SparseCore 0:
  39.4 30.4 reduce-scatter.4
  72.6 31.3 reduce-scatter.2
  140.3 14.7 all-gather.4
  164.3 17.0 all-gather.2
where the time goes:
time: 198 us; the launch traced here: 196 us
  blocking collectives  83.4 us (42%)
  local copies, waits for them, and re-layouts  35.7 us (18%)
  waiting for transfers between devices  24.1 us (12%)
  other arithmetic  21.4 us (11%)
  between operations  14.1 us (7%)
  matrix products  8.94 us (5%)
  starting transfers between devices  8.46 us (4%)
    psum x1, blocking collectives, local(): decay_all = lax.psum(padded, 'tm').reshape(tm_count * slab_hours, comps)  35.2 us
    all_to_all x2, blocking collectives, local(): lax.all_to_all(piece, 'tm', split_axis=2, concat_axis=0, tiled=True)  28.1 us
    unnamed x73, local copies, waits for them, and re-layouts  22.7 us
    all_to_all x1, blocking collectives, local(): lax.all_to_all(smoothed_here, 'tm', split_axis=1, concat_axis=2, tiled=True)  20.1 us
    all_to_all x1, waiting for transfers between devices, local(): lax.all_to_all(smoothed_here, 'tm', split_axis=1, concat_axis=2, tiled=True)  12.1 us
    all_to_all x1, waiting for transfers between devices, local(): lax.all_to_all(masked, 'tm', split_axis=1, concat_axis=0, tiled=True)  11.4 us
    unnamed x9, other arithmetic  10.5 us
    dot_general x2, matrix products, local(): jnp.einsum('so,ogy->sgy', loadings, lax.all_gather(rounded, 'state', axis...  4.83 us
  transfers between devices with their start and end apart: 6, of which 3 were waited for; matrix products, arithmetic and copies ran while one was open for 15% of the time, Pallas kernels for 0%

commit v1 on v0

--- a/solution.py
+++ b/solution.py
@@ -48,7 +48,12 @@
         information = lax.psum_scatter(partial, "state", scatter_dimension=0, tiled=True)
         information = information.reshape(information.shape[0], hours, width)
         smoothed_here = smooth_chunk(information, decay_all)
-        smoothed = lax.all_to_all(smoothed_here, "tm", split_axis=1, concat_axis=2, tiled=True)
+        smoothed = jnp.concatenate(
+            lax.all_to_all(
+                jnp.stack(jnp.split(smoothed_here, lax.axis_size("tm"), axis=1)), "tm", 0, 0
+            ),
+            axis=2,
+        )
         rounded = smoothed.astype(jnp.bfloat16)
         fitted = jnp.einsum(
             "so,ogy->sgy",

time: 198 us -> 178 us (0.90)
  blocking collectives: 83.4 us -> 63.3 us
  starting transfers between devices: 8.46 us -> 15.2 us
  local copies, waits for them, and re-layouts: 35.7 us -> 32.4 us
  other arithmetic: 21.4 us -> 19.2 us
    all_to_all x1 -> x0, blocking collectives: 20.1 us -> none  [local(): lax.all_to_all(smoothed_here, 'tm', split_axis=1, concat_axis=2, tiled=True)]
    add x0 -> x4, other arithmetic: none -> 4.35 us  [the longest x2 2.28 us: smooth_chunk(): rate[:, None] * state + (1.0 - rate * rate)[:, None] * filtered[hour]]
    unnamed x73 -> x23, local copies, waits for them, and re-layouts: 22.7 us -> 18.3 us
    all_to_all x1 -> x2, starting transfers between devices: 4.15 us -> 8.29 us  [local(): lax.all_to_all(jnp.stack(jnp.split(smoothed_here, lax.axis_size('tm'), ax...]
    sub x7, other arithmetic: 4.14 us -> 0.04 us  [smooth_chunk(): 1.0 - rate * rate]
    all_to_all x1 -> x2, waiting for transfers between devices: 12.1 us -> 15.2 us  [local(): lax.all_to_all(jnp.stack(jnp.split(smoothed_here, lax.axis_size('tm'), ax...]
    all_to_all x1, waiting for transfers between devices: 11.4 us -> 8.48 us  [local(): lax.all_to_all(masked, 'tm', split_axis=1, concat_axis=0, tiled=True)]
    all_to_all x1, starting transfers between devices: 4.14 us -> 6.73 us  [local(): lax.all_to_all(masked, 'tm', split_axis=1, concat_axis=0, tiled=True)]
  transfers between devices with their start and end apart: 6 -> 7, of which waited for: 3 -> 3; matrix products, arithmetic and copies ran while one was open for 15% -> 21% of each run, Pallas kernels for 0% -> 0%
where the time goes in v1:
time: 178 us; the launch traced here: 177 us
  blocking collectives  63.3 us (36%)
  local copies, waits for them, and re-layouts  32.4 us (18%)
  waiting for transfers between devices  23.7 us (13%)
  other arithmetic  19.2 us (11%)
  starting transfers between devices  15.2 us (9%)
  between operations  14 us (8%)
  matrix products  8.93 us (5%)
    psum x1, blocking collectives, local(): decay_all = lax.psum(padded, 'tm').reshape(tm_count * slab_hours, comps)  35.2 us
    all_to_all x2, blocking collectives, local(): lax.all_to_all(piece, 'tm', split_axis=2, concat_axis=0, tiled=True)  28.1 us
    unnamed x23, local copies, waits for them, and re-layouts  18.3 us
    all_to_all x2, waiting for transfers between devices, local(): lax.all_to_all(jnp.stack(jnp.split(smoothed_here, lax.axis_size('tm'), ax...  15.2 us
    unnamed x14, other arithmetic  8.88 us
    all_to_all x1, waiting for transfers between devices, local(): lax.all_to_all(masked, 'tm', split_axis=1, concat_axis=0, tiled=True)  8.48 us
    all_to_all x2, starting transfers between devices, local(): lax.all_to_all(jnp.stack(jnp.split(smoothed_here, lax.axis_size('tm'), ax...  8.29 us
    all_to_all x1, starting transfers between devices, local(): lax.all_to_all(masked, 'tm', split_axis=1, concat_axis=0, tiled=True)  6.73 us
  transfers between devices with their start and end apart: 7, of which 3 were waited for; matrix products, arithmetic and copies ran while one was open for 21% of the time, Pallas kernels for 0%

profile of v1, /device:TPU:0, one launch (start us, length us, event | category | flops | bytes accessed | tf_op | source)
XLA Modules:
  0.0 176.8 jit_solution(11815488177007322028)
XLA Ops:
  8.1 3.5 %copy.34 = bf16[64,16,256]{0,1,2:T(8,128)(2,1)} copy(bf16[64,16,256]{2,1,0:T(8,128)(2,1)} %param.4) | data formatting | bytes 1048576 | tf_op args[0]
  14.0 1.4 reshape.7085
  15.5 16.1 %all_to_all.58 = bf16[8,2,8192]{2,1,0:T(2,128)(2,1)} all-to-all(bf16[8,2,8192]{2,1,0:T(2,128)(2,1)S(1)} %reshape.7085), channel_id=1, replica_groups=mesh['tm'=8,'state'=4] {'tm'}, dimensions={0} | all-to-all | bytes 524288 | tf_op jit(solution)/shard_map/all_to_all | solution.py:41
  31.6 2.1 %reshape.7086 = bf16[128,16,64]{2,1,0:T(8,128)(2,1)} reshape(bf16[8,2,8192]{2,1,0:T(2,128)(2,1)} %all_to_all.58) | data formatting | bytes 524288
  33.7 2.2 %copy.39 = bf16[8,64,16,16]{1,0,3,2:T(8,128)(2,1)} copy(bf16[8,64,16,16]{1,2,3,0:T(8,128)(2,1)} %bitcast.146) | data formatting | bytes 524288 | tf_op jit(solution)/shard_map/all_to_all | solution.py:41
  35.9 1.4 reshape.7080
  37.3 2.1 %convolution_bitcast_fusion = f32[2048,256]{0,1:T(8,128)} fusion(bf16[512,256]{0,1:T(8,128)(2,1)S(1)} %reshape.7080, bf16[512,2048]{1,0:T(8,128)(2,1)S(1)} %copy-done), kind=kOutput, calls=%fused_computation | convolution fusion | flops 536870912 | bytes 4456448 | tf_op jit(solution)/shard_map/dot_general | solution.py:43
  39.4 1.4 reshape.7087
  40.8 12.1 %all_to_all.59 = bf16[8,2,8192]{2,1,0:T(2,128)(2,1)} all-to-all(bf16[8,2,8192]{2,1,0:T(2,128)(2,1)S(1)} %reshape.7087), channel_id=1, replica_groups=mesh['tm'=8,'state'=4] {'tm'}, dimensions={0} | all-to-all | bytes 524288 | tf_op jit(solution)/shard_map/all_to_all | solution.py:41
  52.9 2.1 %reshape.7088 = bf16[128,16,64]{2,1,0:T(8,128)(2,1)} reshape(bf16[8,2,8192]{2,1,0:T(2,128)(2,1)} %all_to_all.59) | data formatting | bytes 524288
  55.0 2.3 %copy.36 = bf16[8,64,16,16]{1,0,3,2:T(8,128)(2,1)} copy(bf16[8,64,16,16]{1,2,3,0:T(8,128)(2,1)} %bitcast.147) | data formatting | bytes 524288 | tf_op jit(solution)/shard_map/all_to_all | solution.py:41
  58.7 2.0 %convolution_bitcast_fusion.1 = f32[2048,256]{0,1:T(8,128)} fusion(bf16[512,256]{0,1:T(8,128)(2,1)S(1)} %reshape.7076, bf16[512,2048]{1,0:T(8,128)(2,1)S(1)} %copy-done), kind=kOutput, calls=%fused_computation.1 | convolution fusion | flops 536870912 | bytes 4456448 | tf_op jit(solution)/shard_map/dot_general | solution.py:43
  61.4 35.2 %psum.7 = f32[16,512]{1,0:T(8,128)S(1)} all-reduce(f32[16,512]{1,0:T(8,128)S(1)} %reshape.7075), channel_id=1, replica_groups=mesh['tm'=8,'state'=4] {'tm'}, use_global_device_ids=true, to_apply=%region_0.0 | all-reduce | flops 8192 | bytes 65536 | tf_op jit(solution)/shard_map/psum | solution.py:35
  104.0 4.1 %all-to-all-start.3 = ((f32[8,512,2,16]{1,3,2,0:T(8,128)}), f32[8,512,2,16]{1,3,2,0:T(8,128)}, u32[]{:S(2)}, u32[]{:S(2)}) async-start(f32[8,512,2,16]{1,3,2,0:T(8,128)} %fusion.31), calls=%async_computation.5 | async-start | bytes 1048576 | tf_op jit(solution)/shard_map/all_to_all | solution.py:52
  113.0 5.5 %all-to-all-done.3 = f32[8,512,2,16]{1,3,2,0:T(8,128)} async-done(((f32[8,512,2,16]{1,3,2,0:T(8,128)}), f32[8,512,2,16]{1,3,2,0:T(8,128)}, u32[]{:S(2)}, u32[]{:S(2)}) %all-to-all-start.3) | async-done | bytes 524320 | tf_op jit(solution)/shard_map/all_to_all | solution.py:52
  123.6 4.1 %all-to-all-start.1 = ((f32[8,512,2,16]{1,3,2,0:T(8,128)}), f32[8,512,2,16]{1,3,2,0:T(8,128)}, u32[]{:S(2)}, u32[]{:S(2)}) async-start(f32[8,512,2,16]{1,3,2,0:T(8,128)} %fusion.23), calls=%async_computation.2 | async-start | bytes 1048576 | tf_op jit(solution)/shard_map/all_to_all | solution.py:52
  127.8 1.6 copy.41
  129.4 9.7 %all-to-all-done.1 = f32[8,512,2,16]{1,3,2,0:T(8,128)} async-done(((f32[8,512,2,16]{1,3,2,0:T(8,128)}), f32[8,512,2,16]{1,3,2,0:T(8,128)}, u32[]{:S(2)}, u32[]{:S(2)}) %all-to-all-start.1) | async-done | bytes 524320 | tf_op jit(solution)/shard_map/all_to_all | solution.py:52
  139.1 6.7 %all-to-all-start.4 = ((bf16[64,16,256]{2,0,1:T(8,128)(2,1)}), bf16[64,16,256]{2,0,1:T(8,128)(2,1)}, u32[]{:S(2)}, u32[]{:S(2)}) async-start(bf16[64,16,256]{2,0,1:T(8,128)(2,1)} %copy.41), calls=%async_computation.6 | async-start | bytes 1048576 | tf_op jit(solution)/shard_map/all_to_all | solution.py:31
  147.7 8.5 %all-to-all-done.4 = bf16[64,16,256]{2,0,1:T(8,128)(2,1)} async-done(((bf16[64,16,256]{2,0,1:T(8,128)(2,1)}), bf16[64,16,256]{2,0,1:T(8,128)(2,1)}, u32[]{:S(2)}, u32[]{:S(2)}) %all-to-all-start.4) | async-done | bytes 524320 | tf_op jit(solution)/shard_map/all_to_all | solution.py:31
  158.1 1.8 %copy.49 = bf16[512,2,128]{0,2,1:T(8,128)(2,1)} copy(bf16[512,2,128]{2,0,1:T(8,128)(2,1)} %get-tuple-element.58) | data formatting | bytes 524288
  161.8 2.3 %copy.45 = f32[512,2,256]{2,1,0:T(2,128)} copy(f32[512,2,256]{0,2,1:T(8,128)} %pad_maximum_fusion) | data formatting | bytes 2097152
  164.0 2.8 %fusion.13 = f32[512,2,128]{0,2,1:T(8,128)} fusion(bf16[2048,2,128]{0,2,1:T(8,128)(2,1)} %all-gather.5.cloned.1.call-done, bf16[512,2048]{1,0:T(8,128)(2,1)S(1)} %copy-done, bf16[512,2,128]{0,2,1:T(8,128)(2,1)S(1)} %copy-done.5), kind=kOutput, calls=%fused_computation.9 | convolution fusion | flops 537133056 | bytes 3932160 | tf_op jit(solution)/shard_map/so,ogy->sgy/dot_general | solution.py:58
  166.9 2.0 %fusion.7 = f32[512,2,128]{0,2,1:T(8,128)S(1)} fusion(bf16[2048,2,128]{0,2,1:T(8,128)(2,1)} %all-gather.3.cloned.1.call-done, bf16[512,2048]{1,0:T(8,128)(2,1)S(1)} %copy-done, bf16[512,2,128]{0,2,1:T(8,128)(2,1)S(1)} %copy-done.4), kind=kOutput, calls=%fused_computation.7 | convolution fusion | flops 537133056 | bytes 3932160 | tf_op jit(solution)/shard_map/so,ogy->sgy/dot_general | solution.py:58
  (72 shorter events, 29.7 us)
Async XLA Ops:
  7.2 30.1 %copy-start = (bf16[512,2048]{1,0:T(8,128)(2,1)S(1)}, bf16[512,2048]{1,0:T(8,128)(2,1)}, u32[]{:S(2)}) copy-start(bf16[512,2048]{1,0:T(8,128)(2,1)} %param.6) | copy-start | bytes 6291460
  7.2 89.6 %reduce-scatter.5.cloned.1.call-start = ((), (), s32[]{:S(2)}) async-start(), calls=%async_computation.8 | async-start | bytes 2621440 | tf_op jit(solution)/shard_map/reduce_scatter | solution.py:48
  39.4 68.9 %reduce-scatter.3.cloned.1.call-start = ((), (), s32[]{:S(2)}) async-start(), calls=%async_computation.7 | async-start | bytes 2621440 | tf_op jit(solution)/shard_map/reduce_scatter | solution.py:48
  60.7 0.7 copy-start.6
  104.0 14.4 %all-to-all-start.3 = ((f32[8,512,2,16]{1,3,2,0:T(8,128)}), f32[8,512,2,16]{1,3,2,0:T(8,128)}, u32[]{:S(2)}, u32[]{:S(2)}) async-start(f32[8,512,2,16]{1,3,2,0:T(8,128)} %fusion.31), calls=%async_computation.5 | async-start | bytes 1048576 | tf_op jit(solution)/shard_map/all_to_all | solution.py:52
  108.2 55.9 %all-gather.5.cloned.1.call-start = ((), (), s32[]{:S(2)}) async-start(), calls=%async_computation.10 | async-start | bytes 1310720 | tf_op jit(solution)/shard_map/all_gather | solution.py:61
  119.5 0.8 copy-start.1
  123.6 15.5 %all-to-all-start.1 = ((f32[8,512,2,16]{1,3,2,0:T(8,128)}), f32[8,512,2,16]{1,3,2,0:T(8,128)}, u32[]{:S(2)}, u32[]{:S(2)}) async-start(f32[8,512,2,16]{1,3,2,0:T(8,128)} %fusion.23), calls=%async_computation.2 | async-start | bytes 1048576 | tf_op jit(solution)/shard_map/all_to_all | solution.py:52
  139.1 17.1 %all-to-all-start.4 = ((bf16[64,16,256]{2,0,1:T(8,128)(2,1)}), bf16[64,16,256]{2,0,1:T(8,128)(2,1)}, u32[]{:S(2)}, u32[]{:S(2)}) async-start(bf16[64,16,256]{2,0,1:T(8,128)(2,1)} %copy.41), calls=%async_computation.6 | async-start | bytes 1048576 | tf_op jit(solution)/shard_map/all_to_all | solution.py:31
  145.8 21.0 %all-gather.3.cloned.1.call-start = ((), (), s32[]{:S(2)}) async-start(), calls=%async_computation.9 | async-start | bytes 1310720 | tf_op jit(solution)/shard_map/all_gather | solution.py:61
  146.9 13.8 %copy-start.2 = (f32[512,2,8,16]{0,3,2,1:T(8,128)S(1)}, f32[512,2,8,16]{0,3,2,1:T(8,128)}, u32[]{:S(2)}) copy-start(f32[512,2,8,16]{0,3,2,1:T(8,128)} %copy-done.1) | copy-start | bytes 1572868
  160.7 3.3 %copy-start.5 = (bf16[512,2,128]{0,2,1:T(8,128)(2,1)S(1)}, bf16[512,2,128]{0,2,1:T(8,128)(2,1)}, u32[]{:S(2)}) copy-start(bf16[512,2,128]{0,2,1:T(8,128)(2,1)} %copy.50) | copy-start | bytes 786436
  164.0 2.8 %copy-start.4 = (bf16[512,2,128]{0,2,1:T(8,128)(2,1)S(1)}, bf16[512,2,128]{0,2,1:T(8,128)(2,1)}, u32[]{:S(2)}) copy-start(bf16[512,2,128]{0,2,1:T(8,128)(2,1)} %copy.49) | copy-start | bytes 786436
  166.9 2.0 %copy-start.3 = (f32[512,2,128]{0,2,1:T(8,128)S(1)}, f32[512,2,128]{0,2,1:T(8,128)}, u32[]{:S(2)}) copy-start(f32[512,2,128]{0,2,1:T(8,128)} %fusion.13) | copy-start | bytes 1572868
Sparse Core Ops, SparseCore 0:
  39.5 30.4 reduce-scatter.4
  72.6 31.3 reduce-scatter.2
  121.2 15.8 all-gather.4
  147.9 18.3 all-gather.2
